TPU v7x, 256 devices: a whole 4x4x8 slice. The times are simulated.
256 devices in a mesh: space: 16 (over x_hi, z), chan: 8 (over y, core), dp: 2 (over x_lo).
Axes of the slice: x: 4 (x_hi: 2, x_lo: 2; x = x_hi * 2 + x_lo), y: 4, z: 8, core: 2. Of those that a mesh axis runs over, the one named last changes fastest.
Arguments:
- inputs: bfloat16 [2, 32, 8, 128, 512], P('dp', 'space', None, 'chan'), may hold values from -6 to 6
- cotangent: bfloat16 [2, 32, 8, 128, 512], P('dp', 'space', None, 'chan'), may hold values from -6 to 6
- weight: bfloat16 [27, 128, 128], P(None, 'chan'), may hold values from -0.109375 to 0.109375
Outputs:
- input_grad: bfloat16 [2, 32, 8, 128, 512], P('dp', 'space', None, 'chan')
- weight_grad: float32 [27, 128, 128], P(None, 'chan')
All inputs are finite; a program needn't handle non-finite values.
Results may differ from a plain program's by a relative error of at most 0.001.
Values may be sent and summed in bfloat16 or wider, within the bound.
No kernel may reach another device: no remote copies, remote signals or barrier semaphores. Data moves between devices by JAX's collectives and lax.ppermute only.
A program may use at most 64 MiB of HBM per device.

v0:
```python
import math
import jax
import jax.numpy as jnp
from jax import lax
from jax.sharding import PartitionSpec as P


def from_behind(value, axis, steps):
    count = lax.axis_size(axis)
    initial, last = (max(0, -steps), min(count, count - steps))
    return lax.ppermute(value, axis, [(source, source + steps) for source in range(initial, last)])


def exchange_sum(value, axis, distance):
    count = lax.axis_size(axis)
    return value + lax.ppermute(value, axis, [(i, i ^ distance) for i in range(count)])


def butterfly_sum(value):
    value = exchange_sum(value, "dp", 1)
    for distance in (1, 8, 2, 4):
        value = exchange_sum(value, "space", distance)
    return value


def shift_cells(block, step_z, step_y):
    zero = jnp.zeros((), block.dtype)
    config = ((0, 0, 0), (0, 0, 0), (step_z, -step_z, 0), (0, 0, 0), (step_y, -step_y, 0))
    return lax.pad(block, zero, config)


def local(inputs, cotangent, weight):
    samples, planes, depth, channels, width = inputs.shape
    outputs = weight.shape[2]
    gathered = lax.all_gather(cotangent, "chan", axis=3, tiled=True)
    lower_plane = from_behind(gathered[:, -1:], "space", 1)
    upper_plane = from_behind(gathered[:, :1], "space", -1)
    stacked = jnp.concatenate(
        [shift_cells(inputs, -step_z, -step_y) for step_z in (-1, 0, 1) for step_y in (-1, 0, 1)],
        axis=3,
    )
    accum = jnp.zeros(inputs.shape, jnp.float32)
    groups = []
    for step_x in (-1, 0, 1):
        if step_x == 1:
            slab = jnp.concatenate([lower_plane, gathered[:, : planes - 1]], axis=1)
        elif step_x == -1:
            slab = jnp.concatenate([gathered[:, 1:], upper_plane], axis=1)
        else:
            slab = gathered
        first = 9 * (step_x + 1)
        groups.append(
            jnp.einsum("bxzky,bxzcy->kc", stacked, slab, preferred_element_type=jnp.float32)
        )
        for step_y in (-1, 0, 1):
            kernel = weight[first + step_y + 1 : first + 9 : 3].reshape(3 * channels, outputs)
            product = jnp.einsum(
                "bxzcy,kc->bxzky", slab, kernel, preferred_element_type=jnp.float32
            )
            for place, step_z in enumerate((-1, 0, 1)):
                part = product[:, :, :, place * channels : (place + 1) * channels]
                accum = accum + shift_cells(part, step_z, step_y)
    input_grad = accum.astype(jnp.bfloat16)
    local_grad = jnp.concatenate(groups, axis=0).reshape(27, channels, outputs)
    count = samples * lax.axis_size("dp") * planes * lax.axis_size("space") * depth * width
    scale = 1.0 / math.sqrt(count)
    weight_grad = butterfly_sum(local_grad) * scale
    return (input_grad, weight_grad)


def solution(mesh):
    placed = (
        P("dp", "space", None, "chan", None),
        P("dp", "space", None, "chan", None),
        P(None, "chan", None),
    )
    return jax.shard_map(
        local,
        mesh=mesh,
        in_specs=placed,
        out_specs=(P("dp", "space", None, "chan", None), P(None, "chan", None)),
        check_vma=False,
    )
```

profile of v0, /device:TPU:4, one launch (start us, length us, event | category | flops | bytes accessed | tf_op | source)
XLA Modules:
  0.0 135.7 jit_solution(2542420532690271903)
XLA Ops:
  7.2 0.0 copy-start.1
  7.2 0.0 all-gather.2.cloned.1.call-start
  7.2 0.7 all-gather.2.cloned.1.call-update
  7.9 1.1 fusion.64
  9.0 0.0 copy-start.2
  9.0 1.0 fusion.60
  10.0 1.1 fusion.65
  11.1 1.1 fusion.62
  12.2 0.0 copy-done.1
  12.2 0.1 fusion.63
  12.4 0.1 fusion.66
  12.5 0.1 fusion.67
  12.7 0.0 copy-done.2
  12.7 28.0 %all-gather.2.cloned.1.call-done = bf16[1,2,8,128,512]{4,3,2,1,0:T(8,128)(2,1)} async-done(((bf16[1,2,8,16,512]{4,3,2,1,0:T(8,128)(2,1)}), bf16[1,2,8,128,512]{4,3,2,1,0:T(8,128)(2,1)}) %all-gather.2.cloned.1.call-update) | async-done | bytes 2097168 | tf_op jit(solution)/shard_map/all_gather | solution.py:35
  40.7 0.0 copy-start
  40.7 1.9 %fusion.68 = (bf16[1,1,8,128,512]{4,3,2,1,0:T(8,128)(2,1)S(1)}, bf16[1,1,8,128,512]{4,3,2,1,0:T(8,128)(2,1)S(1)}) fusion(bf16[1,2,8,128,512]{4,3,2,1,0:T(8,128)(2,1)} %all-gather.2.cloned.1.call-done), kind=kLoop, calls=%fused_computation.97 | loop fusion | bytes 4194304 | tf_op jit(solution)/shard_map/slice | solution.py:48
  42.6 5.2 %collective-permute-start = (bf16[1,1,8,128,512]{4,3,2,1,0:T(8,128)(2,1)S(1)}, bf16[1,1,8,128,512]{4,3,2,1,0:T(8,128)(2,1)S(1)}, u32[]{:S(2)}, u32[]{:S(2)}) collective-permute-start(bf16[1,1,8,128,512]{4,3,2,1,0:T(8,128)(2,1)S(1)} %get-tuple-element.3), channel_id=1, source_target_pairs={{16,0},{32,16},{48,32},{64,48},{80,64},{96,80},{112,96},{128,112},... | collective-permute-start | bytes 3145736 | tf_op jit(solution)/shard_map/ppermute | solution.py:11
  47.8 1.9 %collective-permute-start.1 = (bf16[1,1,8,128,512]{4,3,2,1,0:T(8,128)(2,1)S(1)}, bf16[1,1,8,128,512]{4,3,2,1,0:T(8,128)(2,1)S(1)}, u32[]{:S(2)}, u32[]{:S(2)}) collective-permute-start(bf16[1,1,8,128,512]{4,3,2,1,0:T(8,128)(2,1)S(1)} %get-tuple-element.2), channel_id=1, source_target_pairs={{0,16},{16,32},{32,48},{48,64},{64,80},{80,96},{96,112},{112,128},... | collective-permute-start | bytes 3145736 | tf_op jit(solution)/shard_map/ppermute | solution.py:11
  49.7 0.0 copy-done
  49.7 0.4 fusion.19
  50.1 0.1 fusion.74
  50.3 0.4 fusion.16
  50.7 0.4 fusion.13
  51.1 0.4 fusion.72
  51.5 0.8 fusion.25
  52.3 18.3 %collective-permute-done = bf16[1,1,8,128,512]{4,3,2,1,0:T(8,128)(2,1)S(1)} collective-permute-done((bf16[1,1,8,128,512]{4,3,2,1,0:T(8,128)(2,1)S(1)}, bf16[1,1,8,128,512]{4,3,2,1,0:T(8,128)(2,1)S(1)}, u32[]{:S(2)}, u32[]{:S(2)}) %collective-permute-start) | collective-permute-done | bytes 1048608 | tf_op jit(solution)/shard_map/ppermute | solution.py:11
  70.6 0.8 fusion.22
  71.3 7.1 %collective-permute-done.1 = bf16[1,1,8,128,512]{4,3,2,1,0:T(8,128)(2,1)S(1)} collective-permute-done((bf16[1,1,8,128,512]{4,3,2,1,0:T(8,128)(2,1)S(1)}, bf16[1,1,8,128,512]{4,3,2,1,0:T(8,128)(2,1)S(1)}, u32[]{:S(2)}, u32[]{:S(2)}) %collective-permute-start.1) | collective-permute-done | bytes 1048608 | tf_op jit(solution)/shard_map/ppermute | solution.py:11
  78.4 0.8 fusion.30
  79.2 2.2 %collective-permute-start.2 = (f32[27,16,128]{2,1,0:T(8,128)S(1)}, f32[27,16,128]{2,1,0:T(8,128)S(1)}, u32[]{:S(2)}, u32[]{:S(2)}) collective-permute-start(f32[27,16,128]{2,1,0:T(8,128)S(1)} %bitcast.157), channel_id=1, source_target_pairs={{0,1},{1,0},{2,3},{3,2},{4,5},{5,4},{6,7},{7,6},{8,9},{9,8},{10,11... | collective-permute-start | bytes 663560 | tf_op jit(solution)/shard_map/ppermute | solution.py:16
  81.4 0.4 convolution_bitcast_fusion.4
  81.8 0.4 convolution_bitcast_fusion.5
  82.2 0.4 fusion.69
  82.6 0.4 convolution_bitcast_fusion.1
  83.1 0.4 convolution_bitcast_fusion.2
  83.5 2.5 %collective-permute-done.2 = f32[27,16,128]{2,1,0:T(8,128)S(1)} collective-permute-done((f32[27,16,128]{2,1,0:T(8,128)S(1)}, f32[27,16,128]{2,1,0:T(8,128)S(1)}, u32[]{:S(2)}, u32[]{:S(2)}) %collective-permute-start.2) | collective-permute-done | bytes 221216 | tf_op jit(solution)/shard_map/ppermute | solution.py:16
  86.0 0.1 collective-permute-start.3
  86.1 0.4 fusion.75
  86.5 0.4 convolution_bitcast_fusion.3
  87.0 5.1 %collective-permute-done.3 = f32[27,16,128]{2,1,0:T(8,128)S(1)} collective-permute-done((f32[27,16,128]{2,1,0:T(8,128)S(1)}, f32[27,16,128]{2,1,0:T(8,128)S(1)}, u32[]{:S(2)}, u32[]{:S(2)}) %collective-permute-start.3) | collective-permute-done | bytes 221216 | tf_op jit(solution)/shard_map/ppermute | solution.py:16
  92.1 0.1 collective-permute-start.4
  92.2 0.1 fusion.71
  92.3 0.4 convolution_bitcast_fusion
  92.7 6.9 %collective-permute-done.4 = f32[27,16,128]{2,1,0:T(8,128)S(1)} collective-permute-done((f32[27,16,128]{2,1,0:T(8,128)S(1)}, f32[27,16,128]{2,1,0:T(8,128)S(1)}, u32[]{:S(2)}, u32[]{:S(2)}) %collective-permute-start.4) | collective-permute-done | bytes 221216 | tf_op jit(solution)/shard_map/ppermute | solution.py:16
  99.6 0.1 collective-permute-start.5
  99.7 0.1 fusion.77
  99.8 18.3 %collective-permute-done.5 = f32[27,16,128]{2,1,0:T(8,128)S(1)} collective-permute-done((f32[27,16,128]{2,1,0:T(8,128)S(1)}, f32[27,16,128]{2,1,0:T(8,128)S(1)}, u32[]{:S(2)}, u32[]{:S(2)}) %collective-permute-start.5) | collective-permute-done | bytes 221216 | tf_op jit(solution)/shard_map/ppermute | solution.py:16
  118.2 0.1 collective-permute-start.6
  118.3 3.4 %fusion.59 = bf16[1,2,8,16,512]{4,3,2,1,0:T(8,128)(2,1)} fusion(f32[1,2,8,16,512]{4,3,2,1,0:T(8,128)S(1)} %get-tuple-element.26, f32[1,2,8,16,512]{4,3,2,1,0:T(8,128)S(1)} %get-tuple-element.27, f32[1,2,8,16,512]{4,3,2,1,0:T(8,128)S(1)} %get-tuple-element.25, f32[1,2,8,16,512]{4,3,2,1,0:T(8,128)S(1)} %get-tuple-element.41, ...), kind=kLoop, calls=%fused_computation.77 | loop fusion | flops 3538944 | bytes 14417920 | tf_op jit(solution)/shard_map/convert_element_type | solution.py:63
  121.7 6.4 %collective-permute-done.6 = f32[27,16,128]{2,1,0:T(8,128)S(1)} collective-permute-done((f32[27,16,128]{2,1,0:T(8,128)S(1)}, f32[27,16,128]{2,1,0:T(8,128)S(1)}, u32[]{:S(2)}, u32[]{:S(2)}) %collective-permute-start.6) | collective-permute-done | bytes 221216 | tf_op jit(solution)/shard_map/ppermute | solution.py:16
  128.1 0.7 add_multiply_fusion
  (8 shorter events, 0.2 us)
Async XLA Ops:
  7.2 5.0 %copy-start.1 = (bf16[1,2,8,16,512]{4,3,2,1,0:T(8,128)(2,1)S(1)}, bf16[1,2,8,16,512]{4,3,2,1,0:T(8,128)(2,1)}, u32[]{:S(2)}) copy-start(bf16[1,2,8,16,512]{4,3,2,1,0:T(8,128)(2,1)} %param.3) | copy-start | bytes 786436
  7.2 33.5 %all-gather.2.cloned.1.call-start = ((), (), s32[]{:S(2)}) async-start(), calls=%async_computation | async-start | bytes 2359296 | tf_op jit(solution)/shard_map/all_gather | solution.py:35
  9.0 3.7 %copy-start.2 = (bf16[27,16,128]{2,1,0:T(8,128)(2,1)S(1)}, bf16[27,16,128]{2,1,0:T(8,128)(2,1)}, u32[]{:S(2)}) copy-start(bf16[27,16,128]{2,1,0:T(8,128)(2,1)} %param.5) | copy-start | bytes 331780
  40.7 9.0 %copy-start = (bf16[1,2,8,128,512]{4,3,2,1,0:T(8,128)(2,1)S(1)}, bf16[1,2,8,128,512]{4,3,2,1,0:T(8,128)(2,1)}, u32[]{:S(2)}) copy-start(bf16[1,2,8,128,512]{4,3,2,1,0:T(8,128)(2,1)} %all-gather.2.cloned.1.call-done) | copy-start | bytes 6291460
  42.6 28.0 %collective-permute-start = (bf16[1,1,8,128,512]{4,3,2,1,0:T(8,128)(2,1)S(1)}, bf16[1,1,8,128,512]{4,3,2,1,0:T(8,128)(2,1)S(1)}, u32[]{:S(2)}, u32[]{:S(2)}) collective-permute-start(bf16[1,1,8,128,512]{4,3,2,1,0:T(8,128)(2,1)S(1)} %get-tuple-element.3), channel_id=1, source_target_pairs={{16,0},{32,16},{48,32},{64,48},{80,64},{96,80},{112,96},{128,112},... | collective-permute-start | bytes 3145736 | tf_op jit(solution)/shard_map/ppermute | solution.py:11
  47.8 30.6 %collective-permute-start.1 = (bf16[1,1,8,128,512]{4,3,2,1,0:T(8,128)(2,1)S(1)}, bf16[1,1,8,128,512]{4,3,2,1,0:T(8,128)(2,1)S(1)}, u32[]{:S(2)}, u32[]{:S(2)}) collective-permute-start(bf16[1,1,8,128,512]{4,3,2,1,0:T(8,128)(2,1)S(1)} %get-tuple-element.2), channel_id=1, source_target_pairs={{0,16},{16,32},{32,48},{48,64},{64,80},{80,96},{96,112},{112,128},... | collective-permute-start | bytes 3145736 | tf_op jit(solution)/shard_map/ppermute | solution.py:11
  79.2 6.8 %collective-permute-start.2 = (f32[27,16,128]{2,1,0:T(8,128)S(1)}, f32[27,16,128]{2,1,0:T(8,128)S(1)}, u32[]{:S(2)}, u32[]{:S(2)}) collective-permute-start(f32[27,16,128]{2,1,0:T(8,128)S(1)} %bitcast.157), channel_id=1, source_target_pairs={{0,1},{1,0},{2,3},{3,2},{4,5},{5,4},{6,7},{7,6},{8,9},{9,8},{10,11... | collective-permute-start | bytes 663560 | tf_op jit(solution)/shard_map/ppermute | solution.py:16
  86.0 6.0 %collective-permute-start.3 = (f32[27,16,128]{2,1,0:T(8,128)S(1)}, f32[27,16,128]{2,1,0:T(8,128)S(1)}, u32[]{:S(2)}, u32[]{:S(2)}) collective-permute-start(f32[27,16,128]{2,1,0:T(8,128)S(1)} %add.183), channel_id=1, source_target_pairs={{0,16},{16,0},{32,48},{48,32},{64,80},{80,64},{96,112},{112,96},{1... | collective-permute-start | bytes 663560 | tf_op jit(solution)/shard_map/ppermute | solution.py:16
  92.1 7.5 %collective-permute-start.4 = (f32[27,16,128]{2,1,0:T(8,128)S(1)}, f32[27,16,128]{2,1,0:T(8,128)S(1)}, u32[]{:S(2)}, u32[]{:S(2)}) collective-permute-start(f32[27,16,128]{2,1,0:T(8,128)S(1)} %add.184), channel_id=1, source_target_pairs={{0,128},{16,144},{32,160},{48,176},{64,192},{80,208},{96,224},{112... | collective-permute-start | bytes 663560 | tf_op jit(solution)/shard_map/ppermute | solution.py:16
  99.6 18.6 %collective-permute-start.5 = (f32[27,16,128]{2,1,0:T(8,128)S(1)}, f32[27,16,128]{2,1,0:T(8,128)S(1)}, u32[]{:S(2)}, u32[]{:S(2)}) collective-permute-start(f32[27,16,128]{2,1,0:T(8,128)S(1)} %add.185), channel_id=1, source_target_pairs={{0,32},{16,48},{32,0},{48,16},{64,96},{80,112},{96,64},{112,80},{1... | collective-permute-start | bytes 663560 | tf_op jit(solution)/shard_map/ppermute | solution.py:16
  118.2 9.9 %collective-permute-start.6 = (f32[27,16,128]{2,1,0:T(8,128)S(1)}, f32[27,16,128]{2,1,0:T(8,128)S(1)}, u32[]{:S(2)}, u32[]{:S(2)}) collective-permute-start(f32[27,16,128]{2,1,0:T(8,128)S(1)} %add.186), channel_id=1, source_target_pairs={{0,64},{16,80},{32,96},{48,112},{64,0},{80,16},{96,32},{112,48},{1... | collective-permute-start | bytes 663560 | tf_op jit(solution)/shard_map/ppermute | solution.py:16
Sparse Core Ops, SparseCore 0:
  9.8 30.7 all-gather.1
where the time goes:
time: 136 us
  waiting for transfers between devices  93.1 us (68%)
  between operations  14.3 us (11%)
  starting transfers between devices  9.7 us (7%)
  local copies, waits for them, and re-layouts  8.23 us (6%)
  matrix products  6.09 us (4%)
  other arithmetic  4.23 us (3%)
    ppermute x5, waiting for transfers between devices, exchange_sum(): lax.ppermute(value, axis, [(i, i ^ distance) for i in range(count)])  39.2 us
    all_gather x1, waiting for transfers between devices, local(): gathered = lax.all_gather(cotangent, 'chan', axis=3, tiled=True)  28 us
    ppermute x2, waiting for transfers between devices, from_behind(): lax.ppermute(value, axis, [(source, source + steps) for source in range(i...  25.3 us
    ppermute x2, starting transfers between devices, from_behind(): lax.ppermute(value, axis, [(source, source + steps) for source in range(i...  7.13 us
    unnamed x14, local copies, waits for them, and re-layouts  4.55 us
    dot_general x9, matrix products, local(): jnp.einsum('bxzcy,kc->bxzky', slab, kernel, preferred_element_type=jnp.fl...  3.78 us
    convert_element_type x1, other arithmetic, local(): input_grad = accum.astype(jnp.bfloat16)  3.38 us
  transfers between devices with their start and end apart: 8, of which 8 were waited for; matrix products, arithmetic and copies ran while one was open for 11% of the time, Pallas kernels for 0%

commit v1 on v0

--- a/solution.py
+++ b/solution.py
@@ -3,6 +3,16 @@
 import jax.numpy as jnp
 from jax import lax
 from jax.sharding import PartitionSpec as P
+
+
+def part_stops_all(dev_axis, here_x):
+    r2 = jnp.concatenate(
+        jax.lax.all_to_all(
+            jnp.stack([here_x for _ in range(jax.lax.axis_size(dev_axis))], axis=0), dev_axis, 0, 0
+        ),
+        axis=3,
+    )
+    return r2
 
 
 def from_behind(value, axis, steps):
@@ -32,7 +42,7 @@
 def local(inputs, cotangent, weight):
     samples, planes, depth, channels, width = inputs.shape
     outputs = weight.shape[2]
-    gathered = lax.all_gather(cotangent, "chan", axis=3, tiled=True)
+    gathered = part_stops_all("chan", cotangent)
     lower_plane = from_behind(gathered[:, -1:], "space", 1)
     upper_plane = from_behind(gathered[:, :1], "space", -1)
     stacked = jnp.concatenate(

time: 136 us -> 116 us (0.85)
  the two profiles are of different devices: /device:TPU:4 before, /device:TPU:224 now
where the time goes in v1:
time: 116 us
  waiting for transfers between devices  83.5 us (72%)
  starting transfers between devices  12.9 us (11%)
  local copies, waits for them, and re-layouts  8.22 us (7%)
  matrix products  6.09 us (5%)
  other arithmetic  4.21 us (4%)
    ppermute x5, waiting for transfers between devices, exchange_sum(): lax.ppermute(value, axis, [(i, i ^ distance) for i in range(count)])  37.1 us
    all_to_all x1, waiting for transfers between devices, part_stops_all(): jax.lax.all_to_all(jnp.stack([here_x for _ in range(jax.lax.axis_size(dev...  24.8 us
    ppermute x2, waiting for transfers between devices, from_behind(): lax.ppermute(value, axis, [(source, source + steps) for source in range(i...  21.6 us
    ppermute x2, starting transfers between devices, from_behind(): lax.ppermute(value, axis, [(source, source + steps) for source in range(i...  5.84 us
    all_to_all x1, starting transfers between devices, part_stops_all(): jax.lax.all_to_all(jnp.stack([here_x for _ in range(jax.lax.axis_size(dev...  4.6 us
    dot_general x9, matrix products, local(): jnp.einsum('bxzcy,kc->bxzky', slab, kernel, preferred_element_type=jnp.fl...  3.8 us
    unnamed x16, local copies, waits for them, and re-layouts  3.37 us
    convert_element_type x1, other arithmetic, local(): input_grad = accum.astype(jnp.bfloat16)  3.37 us
  transfers between devices with their start and end apart: 8, of which 8 were waited for; matrix products, arithmetic and copies ran while one was open for 10% of the time, Pallas kernels for 0%

profile of v1, /device:TPU:224, one launch (start us, length us, event | category | flops | bytes accessed | tf_op | source)
XLA Modules:
  0.0 115.8 jit_solution(2701968775409882286)
XLA Ops:
  0.6 2.5 %stack.2 = bf16[8,1,2,8,16,512]{5,4,3,2,1,0:T(8,128)(2,1)} broadcast(bf16[2,8,16,512]{3,2,1,0:T(8,128)(2,1)} %bitcast.156), dimensions={2,3,4,5} | broadcast | bytes 2359296 | tf_op jit(solution)/shard_map/stack | solution.py:11
  3.2 0.0 copy-start
  3.2 4.6 %all-to-all-start = ((bf16[8,1,2,8,16,512]{5,4,3,2,1,0:T(8,128)(2,1)}), bf16[8,1,2,8,16,512]{5,4,3,2,1,0:T(8,128)(2,1)S(1)}, u32[]{:S(2)}, u32[]{:S(2)}) async-start(bf16[8,1,2,8,16,512]{5,4,3,2,1,0:T(8,128)(2,1)} %stack.2), calls=%async_computation | async-start | bytes 4194304 | tf_op jit(solution)/shard_map/all_to_all | solution.py:10
  7.8 0.0 copy-done
  7.8 0.1 fusion.46
  7.9 0.0 copy-start.3
  8.0 0.1 fusion.47
  8.1 0.1 fusion.44
  8.3 0.1 fusion.45
  8.4 0.1 fusion.48
  8.6 0.1 fusion.49
  8.7 0.0 copy-start.1
  8.7 1.4 %copy-done.1 = bf16[1,2,8,144,512]{4,3,2,1,0:T(8,128)(2,1)} copy-done((bf16[1,2,8,144,512]{4,3,2,1,0:T(8,128)(2,1)}, bf16[1,2,8,144,512]{4,3,2,1,0:T(8,128)(2,1)S(1)}, u32[]{:S(2)}) %copy-start.1) | copy-done | bytes 2359320
  10.1 0.0 copy-done.3
  10.1 24.8 %all-to-all-done = bf16[8,1,2,8,16,512]{5,4,3,2,1,0:T(8,128)(2,1)S(1)} async-done(((bf16[8,1,2,8,16,512]{5,4,3,2,1,0:T(8,128)(2,1)}), bf16[8,1,2,8,16,512]{5,4,3,2,1,0:T(8,128)(2,1)S(1)}, u32[]{:S(2)}, u32[]{:S(2)}) %all-to-all-start) | async-done | bytes 2097184 | tf_op jit(solution)/shard_map/all_to_all | solution.py:10
  34.9 0.2 copy.5
  35.1 0.2 fusion.50
  35.3 1.9 %collective-permute-start.1 = (bf16[1,1,8,128,512]{4,3,2,1,0:T(8,128)(2,1)S(1)}, bf16[1,1,8,128,512]{4,3,2,1,0:T(8,128)(2,1)S(1)}, u32[]{:S(2)}, u32[]{:S(2)}) collective-permute-start(bf16[1,1,8,128,512]{4,3,2,1,0:T(8,128)(2,1)S(1)} %get-tuple-element.2), channel_id=1, source_target_pairs={{0,16},{16,32},{32,48},{48,64},{64,80},{80,96},{96,112},{112,128},... | collective-permute-start | bytes 3145736 | tf_op jit(solution)/shard_map/ppermute | solution.py:21
  37.3 3.9 %collective-permute-start = (bf16[1,1,8,128,512]{4,3,2,1,0:T(8,128)(2,1)S(1)}, bf16[1,1,8,128,512]{4,3,2,1,0:T(8,128)(2,1)S(1)}, u32[]{:S(2)}, u32[]{:S(2)}) collective-permute-start(bf16[1,1,8,128,512]{4,3,2,1,0:T(8,128)(2,1)S(1)} %get-tuple-element.3), channel_id=1, source_target_pairs={{16,0},{32,16},{48,32},{64,48},{80,64},{96,80},{112,96},{128,112},... | collective-permute-start | bytes 3145736 | tf_op jit(solution)/shard_map/ppermute | solution.py:21
  41.2 0.4 convolution_bitcast_fusion.6
  41.6 0.1 fusion.56
  41.7 0.4 convolution_bitcast_fusion.7
  42.2 0.4 convolution_bitcast_fusion.8
  42.6 0.0 copy-start.2
  42.6 0.4 fusion.54
  43.0 1.2 %copy-done.2 = bf16[1,2,8,144,512]{4,3,2,1,0:T(8,128)(2,1)S(1)} copy-done((bf16[1,2,8,144,512]{4,3,2,1,0:T(8,128)(2,1)S(1)}, bf16[1,2,8,144,512]{4,3,2,1,0:T(8,128)(2,1)}, u32[]{:S(2)}) %copy-start.2) | copy-done | bytes 2359320
  44.3 0.8 fusion.9
  45.0 16.8 %collective-permute-done.1 = bf16[1,1,8,128,512]{4,3,2,1,0:T(8,128)(2,1)S(1)} collective-permute-done((bf16[1,1,8,128,512]{4,3,2,1,0:T(8,128)(2,1)S(1)}, bf16[1,1,8,128,512]{4,3,2,1,0:T(8,128)(2,1)S(1)}, u32[]{:S(2)}, u32[]{:S(2)}) %collective-permute-start.1) | collective-permute-done | bytes 1048608 | tf_op jit(solution)/shard_map/ppermute | solution.py:21
  61.8 0.8 fusion.12
  62.6 4.8 %collective-permute-done = bf16[1,1,8,128,512]{4,3,2,1,0:T(8,128)(2,1)S(1)} collective-permute-done((bf16[1,1,8,128,512]{4,3,2,1,0:T(8,128)(2,1)S(1)}, bf16[1,1,8,128,512]{4,3,2,1,0:T(8,128)(2,1)S(1)}, u32[]{:S(2)}, u32[]{:S(2)}) %collective-permute-start) | collective-permute-done | bytes 1048608 | tf_op jit(solution)/shard_map/ppermute | solution.py:21
  67.4 0.8 fusion.6
  68.2 1.6 %collective-permute-start.2 = (f32[27,16,128]{2,1,0:T(8,128)S(1)}, f32[27,16,128]{2,1,0:T(8,128)S(1)}, u32[]{:S(2)}, u32[]{:S(2)}) collective-permute-start(f32[27,16,128]{2,1,0:T(8,128)S(1)} %bitcast.154), channel_id=1, source_target_pairs={{0,1},{1,0},{2,3},{3,2},{4,5},{5,4},{6,7},{7,6},{8,9},{9,8},{10,11... | collective-permute-start | bytes 663560 | tf_op jit(solution)/shard_map/ppermute | solution.py:26
  69.9 0.4 convolution_bitcast_fusion.4
  70.3 0.4 convolution_bitcast_fusion.5
  70.7 0.4 fusion.51
  71.1 0.4 convolution_bitcast_fusion.1
  71.6 0.4 convolution_bitcast_fusion.2
  72.0 2.3 %collective-permute-done.2 = f32[27,16,128]{2,1,0:T(8,128)S(1)} collective-permute-done((f32[27,16,128]{2,1,0:T(8,128)S(1)}, f32[27,16,128]{2,1,0:T(8,128)S(1)}, u32[]{:S(2)}, u32[]{:S(2)}) %collective-permute-start.2) | collective-permute-done | bytes 221216 | tf_op jit(solution)/shard_map/ppermute | solution.py:26
  74.3 0.1 collective-permute-start.3
  74.4 0.4 fusion.57
  74.8 0.4 convolution_bitcast_fusion.3
  75.3 5.1 %collective-permute-done.3 = f32[27,16,128]{2,1,0:T(8,128)S(1)} collective-permute-done((f32[27,16,128]{2,1,0:T(8,128)S(1)}, f32[27,16,128]{2,1,0:T(8,128)S(1)}, u32[]{:S(2)}, u32[]{:S(2)}) %collective-permute-start.3) | collective-permute-done | bytes 221216 | tf_op jit(solution)/shard_map/ppermute | solution.py:26
  80.4 0.5 collective-permute-start.4
  80.9 0.2 fusion.53
  81.1 0.4 convolution_bitcast_fusion
  81.5 6.4 %collective-permute-done.4 = f32[27,16,128]{2,1,0:T(8,128)S(1)} collective-permute-done((f32[27,16,128]{2,1,0:T(8,128)S(1)}, f32[27,16,128]{2,1,0:T(8,128)S(1)}, u32[]{:S(2)}, u32[]{:S(2)}) %collective-permute-start.4) | collective-permute-done | bytes 221216 | tf_op jit(solution)/shard_map/ppermute | solution.py:26
  87.9 0.1 collective-permute-start.5
  88.0 0.2 fusion.59
  88.2 16.9 %collective-permute-done.5 = f32[27,16,128]{2,1,0:T(8,128)S(1)} collective-permute-done((f32[27,16,128]{2,1,0:T(8,128)S(1)}, f32[27,16,128]{2,1,0:T(8,128)S(1)}, u32[]{:S(2)}, u32[]{:S(2)}) %collective-permute-start.5) | collective-permute-done | bytes 221216 | tf_op jit(solution)/shard_map/ppermute | solution.py:26
  105.1 0.1 collective-permute-start.6
  105.2 3.4 %fusion.41 = bf16[1,2,8,16,512]{4,3,2,1,0:T(8,128)(2,1)} fusion(f32[1,2,8,16,512]{4,3,2,1,0:T(8,128)S(1)} %get-tuple-element.26, f32[1,2,8,16,512]{4,3,2,1,0:T(8,128)S(1)} %get-tuple-element.27, f32[1,2,8,16,512]{4,3,2,1,0:T(8,128)S(1)} %get-tuple-element.25, f32[1,2,8,16,512]{4,3,2,1,0:T(8,128)S(1)} %get-tuple-element.41, ...), kind=kLoop, calls=%fused_computation.70 | loop fusion | flops 3538944 | bytes 14417920 | tf_op jit(solution)/shard_map/convert_element_type | solution.py:73
  108.6 6.5 %collective-permute-done.6 = f32[27,16,128]{2,1,0:T(8,128)S(1)} collective-permute-done((f32[27,16,128]{2,1,0:T(8,128)S(1)}, f32[27,16,128]{2,1,0:T(8,128)S(1)}, u32[]{:S(2)}, u32[]{:S(2)}) %collective-permute-start.6) | collective-permute-done | bytes 221216 | tf_op jit(solution)/shard_map/ppermute | solution.py:26
  115.0 0.7 add_multiply_fusion
  (9 shorter events, 0.2 us)
Async XLA Ops:
  3.2 4.6 %copy-start = (bf16[1,2,8,16,512]{4,3,2,1,0:T(8,128)(2,1)S(1)}, bf16[1,2,8,16,512]{4,3,2,1,0:T(8,128)(2,1)}, u32[]{:S(2)}) copy-start(bf16[1,2,8,16,512]{4,3,2,1,0:T(8,128)(2,1)} %param.3) | copy-start | bytes 786436
  3.2 31.8 %all-to-all-start = ((bf16[8,1,2,8,16,512]{5,4,3,2,1,0:T(8,128)(2,1)}), bf16[8,1,2,8,16,512]{5,4,3,2,1,0:T(8,128)(2,1)S(1)}, u32[]{:S(2)}, u32[]{:S(2)}) async-start(bf16[8,1,2,8,16,512]{5,4,3,2,1,0:T(8,128)(2,1)} %stack.2), calls=%async_computation | async-start | bytes 4194304 | tf_op jit(solution)/shard_map/all_to_all | solution.py:10
  7.9 2.2 %copy-start.3 = (bf16[27,16,128]{2,1,0:T(8,128)(2,1)S(1)}, bf16[27,16,128]{2,1,0:T(8,128)(2,1)}, u32[]{:S(2)}) copy-start(bf16[27,16,128]{2,1,0:T(8,128)(2,1)} %param.5) | copy-start | bytes 331780
  8.7 1.4 %copy-start.1 = (bf16[1,2,8,144,512]{4,3,2,1,0:T(8,128)(2,1)}, bf16[1,2,8,144,512]{4,3,2,1,0:T(8,128)(2,1)S(1)}, u32[]{:S(2)}) copy-start(bf16[1,2,8,144,512]{4,3,2,1,0:T(8,128)(2,1)S(1)} %fusion.49) | copy-start | bytes 7077892
  35.3 26.5 %collective-permute-start.1 = (bf16[1,1,8,128,512]{4,3,2,1,0:T(8,128)(2,1)S(1)}, bf16[1,1,8,128,512]{4,3,2,1,0:T(8,128)(2,1)S(1)}, u32[]{:S(2)}, u32[]{:S(2)}) collective-permute-start(bf16[1,1,8,128,512]{4,3,2,1,0:T(8,128)(2,1)S(1)} %get-tuple-element.2), channel_id=1, source_target_pairs={{0,16},{16,32},{32,48},{48,64},{64,80},{80,96},{96,112},{112,128},... | collective-permute-start | bytes 3145736 | tf_op jit(solution)/shard_map/ppermute | solution.py:21
  37.3 30.1 %collective-permute-start = (bf16[1,1,8,128,512]{4,3,2,1,0:T(8,128)(2,1)S(1)}, bf16[1,1,8,128,512]{4,3,2,1,0:T(8,128)(2,1)S(1)}, u32[]{:S(2)}, u32[]{:S(2)}) collective-permute-start(bf16[1,1,8,128,512]{4,3,2,1,0:T(8,128)(2,1)S(1)} %get-tuple-element.3), channel_id=1, source_target_pairs={{16,0},{32,16},{48,32},{64,48},{80,64},{96,80},{112,96},{128,112},... | collective-permute-start | bytes 3145736 | tf_op jit(solution)/shard_map/ppermute | solution.py:21
  42.6 1.7 %copy-start.2 = (bf16[1,2,8,144,512]{4,3,2,1,0:T(8,128)(2,1)S(1)}, bf16[1,2,8,144,512]{4,3,2,1,0:T(8,128)(2,1)}, u32[]{:S(2)}) copy-start(bf16[1,2,8,144,512]{4,3,2,1,0:T(8,128)(2,1)} %copy-done.1) | copy-start | bytes 7077892
  68.2 6.1 %collective-permute-start.2 = (f32[27,16,128]{2,1,0:T(8,128)S(1)}, f32[27,16,128]{2,1,0:T(8,128)S(1)}, u32[]{:S(2)}, u32[]{:S(2)}) collective-permute-start(f32[27,16,128]{2,1,0:T(8,128)S(1)} %bitcast.154), channel_id=1, source_target_pairs={{0,1},{1,0},{2,3},{3,2},{4,5},{5,4},{6,7},{7,6},{8,9},{9,8},{10,11... | collective-permute-start | bytes 663560 | tf_op jit(solution)/shard_map/ppermute | solution.py:26
  74.3 6.0 %collective-permute-start.3 = (f32[27,16,128]{2,1,0:T(8,128)S(1)}, f32[27,16,128]{2,1,0:T(8,128)S(1)}, u32[]{:S(2)}, u32[]{:S(2)}) collective-permute-start(f32[27,16,128]{2,1,0:T(8,128)S(1)} %add.183), channel_id=1, source_target_pairs={{0,16},{16,0},{32,48},{48,32},{64,80},{80,64},{96,112},{112,96},{1... | collective-permute-start | bytes 663560 | tf_op jit(solution)/shard_map/ppermute | solution.py:26
  80.4 7.5 %collective-permute-start.4 = (f32[27,16,128]{2,1,0:T(8,128)S(1)}, f32[27,16,128]{2,1,0:T(8,128)S(1)}, u32[]{:S(2)}, u32[]{:S(2)}) collective-permute-start(f32[27,16,128]{2,1,0:T(8,128)S(1)} %add.184), channel_id=1, source_target_pairs={{0,128},{16,144},{32,160},{48,176},{64,192},{80,208},{96,224},{112... | collective-permute-start | bytes 663560 | tf_op jit(solution)/shard_map/ppermute | solution.py:26
  87.9 17.2 %collective-permute-start.5 = (f32[27,16,128]{2,1,0:T(8,128)S(1)}, f32[27,16,128]{2,1,0:T(8,128)S(1)}, u32[]{:S(2)}, u32[]{:S(2)}) collective-permute-start(f32[27,16,128]{2,1,0:T(8,128)S(1)} %add.185), channel_id=1, source_target_pairs={{0,32},{16,48},{32,0},{48,16},{64,96},{80,112},{96,64},{112,80},{1... | collective-permute-start | bytes 663560 | tf_op jit(solution)/shard_map/ppermute | solution.py:26
  105.1 9.9 %collective-permute-start.6 = (f32[27,16,128]{2,1,0:T(8,128)S(1)}, f32[27,16,128]{2,1,0:T(8,128)S(1)}, u32[]{:S(2)}, u32[]{:S(2)}) collective-permute-start(f32[27,16,128]{2,1,0:T(8,128)S(1)} %add.186), channel_id=1, source_target_pairs={{0,64},{16,80},{32,96},{48,112},{64,0},{80,16},{96,32},{112,48},{1... | collective-permute-start | bytes 663560 | tf_op jit(solution)/shard_map/ppermute | solution.py:26
